TPU v7x, 256 devices: a whole 4x4x8 slice. The times are simulated.
256 devices in a mesh: role: 2 (over core), dp: 16 (over x, y), tensor: 8 (over z).
Axes of the slice: x: 4, y: 4, z: 8, core: 2. Of those that a mesh axis runs over, the one named last changes fastest.
Arguments:
- queries: bfloat16 [1024, 128, 576], P(('dp', 'tensor'), 'role'), may hold values from -13 to 13
- latent_cache: bfloat16 [512, 1024, 576], P(('dp', 'tensor')), may hold values from -4 to 4
- new_latent: bfloat16 [1024, 576], P(('dp', 'tensor')), may hold values from -9 to 9
- cache_lengths: int32 [512], P(('dp', 'tensor')), may hold values from 2 to 1024
- value_proj: bfloat16 [128, 512, 128], P(('role', 'tensor')), may hold values from -1 to 1
- out_proj: bfloat16 [16384, 7168], P(('role', 'tensor'), 'dp'), may hold values from -0.046875 to 0.046875
- residual: bfloat16 [1024, 7168], P(('role', 'tensor'), 'dp'), may hold values from -68 to 68
- norm_gain: bfloat16 [7168], replicated, may hold values from 0.5 to 1.5
- routes: int32 [1024, 8], P(('role', 'tensor')), may hold values from 0 to 15, all different within a row; in each aligned block of 64 rows (0 to 63, 64 to 127, ...) at most 40 rows name the same one
- gate_values: float32 [1024, 8], P(('role', 'tensor')), may hold values from 0.2 to 0.8
- tenant_ids: int32 [1024], P(('role', 'tensor')), may hold values from 0 to 2
- expert_gate_weight: bfloat16 [16, 7168, 2048], P('dp', None, ('role', 'tensor')), may hold values from -0.0625 to 0.0625
- expert_up_weight: bfloat16 [16, 7168, 2048], P('dp', None, ('role', 'tensor')), may hold values from -0.0625 to 0.0625
- expert_down_weight: bfloat16 [16, 2048, 7168], P('dp', ('role', 'tensor')), may hold values from -0.125 to 0.125
- left_delta_factor: bfloat16 [3, 16, 2048, 64], P(None, 'dp', ('role', 'tensor')), may hold values from -0.125 to 0.125
- factor_right: bfloat16 [3, 16, 64, 7168], P(None, 'dp'), may hold values from -0.75 to 0.75
Outputs:
- mixed: bfloat16 [1024, 7168], P(('role', 'tensor'), 'dp')
Inputs may be any that keep to these rules, and one draw needn't show every extreme that they name: `routes`: in each aligned block of 64 tokens no expert is named by more than 40 of them.
All inputs are finite; a program needn't handle non-finite values.
Results may differ from a plain program's by a relative error of at most 0.008.
Values may be sent and summed in bfloat16 or wider, within the bound.
No kernel may reach another device: no remote copies, remote signals or barrier semaphores. Data moves between devices by JAX's collectives and lax.ppermute only.
A program may use at most 128 MiB of HBM per device.

v0:
```python
import jax
import jax.numpy as jnp
from jax import lax
from jax.sharding import PartitionSpec as P

LAT = 512
EXPERTS = 16
TEN = 3
SCORE_SCALE = 0.07216878364870323
NORM_EPS = 1e-06
MASKED = -1e30
RT = ("role", "tensor")


def rms_rows(input_rows, norm_gain):
    wide = input_rows.astype(jnp.float32)
    scale = lax.rsqrt(jnp.mean(wide * wide, axis=-1, keepdims=True) + NORM_EPS)
    return (wide * scale * norm_gain.astype(jnp.float32)).astype(jnp.bfloat16)


def slot_table(routes, expert, capacity):
    hit = jnp.any(routes == expert, axis=-1).astype(jnp.int32)
    earlier = jnp.cumsum(hit, axis=-1) - hit
    slot_ids = jnp.arange(capacity, dtype=jnp.int32)
    return (hit[..., None, :] > 0) & (earlier[..., None, :] == slot_ids[:, None])


def local(
    queries,
    latent_cache,
    new_latent,
    cache_lengths,
    value_proj,
    out_proj,
    residual,
    norm_gain,
    routes,
    gate_values,
    tenant_ids,
    expert_gate_weight,
    expert_up_weight,
    expert_down_weight,
    left_delta_factor,
    factor_right,
):
    n_slices = lax.axis_size(RT)
    slice_idx = lax.axis_index(RT)
    group_rows = residual.shape[0]
    capacity = 5 * group_rows // 8
    model_width = expert_down_weight.shape[2]
    col_width = model_width // n_slices
    expert = lax.axis_index("dp")
    labels = jnp.arange(EXPERTS, dtype=jnp.int32)
    table = slot_table(routes, labels[:, None, None], capacity)
    mine = lax.dynamic_index_in_dim(table, expert, 0, keepdims=False)
    mine_owner = jnp.sum(mine.astype(jnp.int32) * tenant_ids[None, :], axis=1)
    hidden_slice = expert_down_weight.shape[1]
    down_local = expert_down_weight[0].reshape(hidden_slice, n_slices, col_width)
    down_local = jnp.transpose(down_local, (1, 0, 2))
    left_local = left_delta_factor[:, 0]
    tenants, _, rank = left_local.shape
    left_local = jnp.transpose(left_local, (1, 0, 2)).reshape(1, hidden_slice, tenants * rank)
    left_local = jnp.broadcast_to(left_local, (n_slices, hidden_slice, tenants * rank))
    down_pack = jnp.concatenate([down_local, left_local], axis=2)
    pack_width = down_pack.shape[2]
    info = mine_owner.astype(jnp.bfloat16)
    info_rows = jnp.zeros((8, pack_width), jnp.bfloat16).at[0, : info.shape[0]].set(info)
    info_rows = jnp.broadcast_to(info_rows[None], (n_slices, 8, pack_width))
    down_pack = jnp.concatenate([down_pack, info_rows], axis=1)
    down_pack = lax.all_to_all(down_pack, RT, split_axis=0, concat_axis=0, tiled=True)
    right_w = lax.dynamic_slice_in_dim(factor_right[:, 0], slice_idx * col_width, col_width, 2)
    seq_count, context, width = latent_cache.shape
    local_heads = queries.shape[1]
    paired = queries.reshape(seq_count, 2, local_heads, width)
    scores = (
        jnp.einsum("sqhd,spd->sqhp", paired, latent_cache, preferred_element_type=jnp.float32)
        * SCORE_SCALE
    )
    present = jnp.arange(context, dtype=jnp.int32)[None, :] < cache_lengths[:, None]
    scores = jnp.where(present[:, None, None, :], scores, MASKED)
    fresh_keys = new_latent.reshape(seq_count, 2, width)
    fresh = (
        jnp.einsum("sqhd,skd->sqhk", paired, fresh_keys, preferred_element_type=jnp.float32)
        * SCORE_SCALE
    )
    causal = jnp.arange(2)[:, None] >= jnp.arange(2)[None, :]
    fresh = jnp.where(causal[None, :, None, :], fresh, MASKED)
    top = jnp.maximum(jnp.max(scores, axis=3), jnp.max(fresh, axis=3))[..., None]
    weights = jnp.exp(scores - top)
    fresh_weights = jnp.exp(fresh - top)
    total = jnp.sum(weights, axis=3) + jnp.sum(fresh_weights, axis=3)
    summed = jnp.einsum(
        "sqhp,spd->sqhd",
        weights.astype(jnp.bfloat16),
        latent_cache[:, :, :LAT],
        preferred_element_type=jnp.float32,
    )
    summed = summed + jnp.einsum(
        "sqhk,skd->sqhd",
        fresh_weights.astype(jnp.bfloat16),
        fresh_keys[:, :, :LAT],
        preferred_element_type=jnp.float32,
    )
    attended = (
        (summed / total[..., None]).astype(jnp.bfloat16).reshape(seq_count * 2, local_heads, LAT)
    )
    by_head = lax.all_to_all(attended, "tensor", split_axis=1, concat_axis=0, tiled=True)
    head_values = jnp.einsum(
        "thl,hlv->thv", by_head, value_proj, preferred_element_type=jnp.float32
    ).astype(jnp.bfloat16)
    head_values = head_values.reshape(
        head_values.shape[0], head_values.shape[1] * head_values.shape[2]
    )
    all_values = lax.all_gather(head_values, "dp", axis=0, tiled=True)
    owners = down_pack[:, hidden_slice, :capacity].astype(jnp.int32).reshape(n_slices * capacity)
    down_pack = down_pack[:, :hidden_slice].reshape(n_slices * hidden_slice, pack_width)
    down_w = down_pack[:, :col_width]
    left_w = down_pack[:, col_width:].reshape(n_slices * hidden_slice, tenants, rank)
    down_w, left_w, owners, all_values = lax.optimization_barrier(
        (down_w, left_w, owners, all_values)
    )
    partial = jnp.dot(all_values, out_proj, preferred_element_type=jnp.float32)
    half = partial.shape[0] // 2
    role_idx = lax.axis_index("role")
    keep = lax.dynamic_slice_in_dim(partial, role_idx * half, half, 0)
    give = lax.dynamic_slice_in_dim(partial, (1 - role_idx) * half, half, 0)
    partial = keep + lax.ppermute(give.astype(jnp.bfloat16), "role", [(0, 1), (1, 0)]).astype(
        jnp.float32
    )
    n_tensor = lax.axis_size("tensor")
    partial = partial.reshape(n_tensor, partial.shape[0] // n_tensor, partial.shape[1])
    partial = lax.all_to_all(
        partial.astype(jnp.bfloat16), "tensor", split_axis=0, concat_axis=0, tiled=True
    )
    attention = jnp.sum(partial.astype(jnp.float32), axis=0)
    mixed_in = lax.optimization_barrier(
        (residual.astype(jnp.float32) + attention).astype(jnp.bfloat16)
    )
    n_dp = lax.axis_size("dp")
    spread = jnp.broadcast_to(mixed_in[None], (n_dp,) + mixed_in.shape)
    full_rows = lax.all_to_all(spread, "dp", split_axis=0, concat_axis=0, tiled=True)
    full_rows = full_rows.reshape(-1, group_rows, mixed_in.shape[1])
    full_rows = jnp.transpose(full_rows, (1, 0, 2)).reshape(group_rows, model_width)
    normed = rms_rows(full_rows, norm_gain)
    picked = jnp.dot(mine.astype(jnp.bfloat16), normed, preferred_element_type=jnp.float32).astype(
        jnp.bfloat16
    )
    collected_rows = lax.all_gather(picked, RT, axis=0, tiled=True)
    gate_scores = jnp.dot(collected_rows, expert_gate_weight[0], preferred_element_type=jnp.float32)
    upper_bound = jnp.dot(collected_rows, expert_up_weight[0], preferred_element_type=jnp.float32)
    hidden = (jax.nn.silu(gate_scores) * upper_bound).astype(jnp.bfloat16)
    gathered = lax.all_gather(hidden, RT, axis=0, tiled=False)
    down_w = down_w.reshape(n_slices, hidden_slice, col_width)
    left_w = left_w.reshape(n_slices, hidden_slice, tenants, rank)
    base_output = jnp.einsum("jsh,jhc->sc", gathered, down_w, preferred_element_type=jnp.float32)
    owner_mask = (owners[:, None] == jnp.arange(TEN, dtype=jnp.int32)[None, :]).astype(jnp.float32)
    mixing = (
        jnp.einsum("jsf,jftr->str", gathered, left_w, preferred_element_type=jnp.float32)
        * owner_mask[:, :, None]
    )
    delta = jnp.einsum(
        "str,trd->sd", mixing, right_w.astype(jnp.float32), precision=lax.Precision.HIGHEST
    )
    expert_out = (base_output - delta).astype(jnp.bfloat16)
    expert_out = expert_out.reshape(n_slices, capacity, col_width)
    by_group = lax.all_to_all(expert_out, RT, split_axis=0, concat_axis=0, tiled=True)
    by_expert = lax.all_to_all(by_group, "dp", split_axis=0, concat_axis=0, tiled=True)
    chosen = (routes[:, :, None] == labels[None, None, :]).astype(jnp.float32)
    gate_of = jnp.sum(gate_values[:, :, None] * chosen, axis=1)
    weighting = table.astype(jnp.float32) * gate_of.T[:, None, :]
    expert_part = jnp.einsum(
        "ecg,ecd->gd", weighting, by_expert.astype(jnp.float32), precision=lax.Precision.HIGHEST
    )
    return (mixed_in.astype(jnp.float32) + expert_part).astype(jnp.bfloat16)


def solution(mesh):
    placed = (
        P(("dp", "tensor"), "role", None),
        P(("dp", "tensor"), None, None),
        P(("dp", "tensor"), None),
        P(("dp", "tensor")),
        P(("role", "tensor"), None, None),
        P(("role", "tensor"), "dp"),
        P(("role", "tensor"), "dp"),
        P(),
        P(("role", "tensor"), None),
        P(("role", "tensor"), None),
        P(("role", "tensor")),
        P("dp", None, ("role", "tensor")),
        P("dp", None, ("role", "tensor")),
        P("dp", ("role", "tensor"), None),
        P(None, "dp", ("role", "tensor"), None),
        P(None, "dp", None, None),
    )
    return jax.shard_map(
        local, mesh=mesh, in_specs=placed, out_specs=P(("role", "tensor"), "dp"), check_vma=False
    )
```

profile of v0, /device:TPU:32, one launch (start us, length us, event | category | flops | bytes accessed | tf_op | source)
XLA Modules:
  0.0 349.5 jit_solution(5170644350469607524)
XLA Ops:
  8.2 3.9 %fusion.8 = (f32[4,2,64]{2,1,0:T(2,128)S(1)}, f32[4,2,64,1024]{3,2,1,0:T(8,128)S(1)}) fusion(pred[4,1024]{1,0:T(4,128)(4,1)S(1)} %iota_compare_fusion.3, bf16[4,2,64,576]{3,2,1,0:T(8,128)(2,1)} %bitcast.125, bf16[4,1024,576]{1,2,0:T(8,128)(2,1)} %param.19), kind=kOutput, calls=%fused_computation.14 | convolution fusion | flops 605552128 | bytes 7411712 | tf_op jit(solution)/shard_map/sqhd,spd->sqhp/dot_general | solution.py:76
  13.2 2.5 fusion.2
  15.8 1.6 fusion.18
  18.5 8.6 %all-to-all-start.1 = ((bf16[8,64,512]{2,0,1:T(8,128)(2,1)}), bf16[8,64,512]{2,0,1:T(8,128)(2,1)S(1)}, u32[]{:S(2)}, u32[]{:S(2)}) async-start(bf16[8,64,512]{2,0,1:T(8,128)(2,1)} %copy.75), calls=%async_computation.1 | async-start | bytes 1048576 | tf_op jit(solution)/shard_map/all_to_all | solution.py:107
  27.7 3.9 %copy.70 = bf16[1,128,7168]{1,2,0:T(8,128)(2,1)} copy(bf16[1,128,7168]{2,1,0:T(8,128)(2,1)} %param.31) | data formatting | bytes 3670016 | tf_op args[13]
  33.1 3.5 pad_maximum_fusion
  36.6 6.3 %copy.72 = bf16[16,136,640]{2,1,0:T(8,128)(2,1)} copy(bf16[16,136,640]{1,2,0:T(8,128)(2,1)} %pad_maximum_fusion) | data formatting | bytes 5570560 | tf_op jit(solution)/shard_map/concatenate | solution.py:69
  43.1 6.9 %all-to-all-start = ((bf16[16,136,640]{2,1,0:T(8,128)(2,1)}), bf16[16,136,640]{2,1,0:T(8,128)(2,1)}, u32[]{:S(2)}, u32[]{:S(2)}) async-start(bf16[16,136,640]{2,1,0:T(8,128)(2,1)} %copy.72), calls=%async_computation | async-start | bytes 5570560 | tf_op jit(solution)/shard_map/all_to_all | solution.py:70
  50.1 1.5 fusion.27
  52.4 60.9 %all-to-all-done = bf16[16,136,640]{2,1,0:T(8,128)(2,1)} async-done(((bf16[16,136,640]{2,1,0:T(8,128)(2,1)}), bf16[16,136,640]{2,1,0:T(8,128)(2,1)}, u32[]{:S(2)}, u32[]{:S(2)}) %all-to-all-start) | async-done | bytes 2785312 | tf_op jit(solution)/shard_map/all_to_all | solution.py:70
  113.2 2.0 slice.40
  118.1 2.2 copy.73
  121.2 3.0 fusion.63
  126.0 1.6 collective-permute-done
  127.6 2.2 add_convert_fusion
  131.0 21.8 %all_to_all.43 = bf16[8,64,448]{2,1,0:T(8,128)(2,1)S(1)} all-to-all(bf16[8,64,448]{2,1,0:T(8,128)(2,1)S(1)} %bitcast.123), channel_id=1, replica_groups=mesh['role'=2,'dp'=16,'tensor'=8] {'tensor'}, dimensions={0} | all-to-all | bytes 917504 | tf_op jit(solution)/shard_map/all_to_all | solution.py:132
  154.6 7.1 %all-to-all-start.3 = ((bf16[16,64,448]{2,1,0:T(8,128)(2,1)}), bf16[16,64,448]{2,1,0:T(8,128)(2,1)}, u32[]{:S(2)}, u32[]{:S(2)}) async-start(bf16[16,64,448]{2,1,0:T(8,128)(2,1)} %broadcast_in_dim.39), calls=%async_computation.3 | async-start | bytes 2097152 | tf_op jit(solution)/shard_map/all_to_all | solution.py:141
  162.0 14.8 %all-to-all-done.3 = bf16[16,64,448]{2,1,0:T(8,128)(2,1)} async-done(((bf16[16,64,448]{2,1,0:T(8,128)(2,1)}), bf16[16,64,448]{2,1,0:T(8,128)(2,1)}, u32[]{:S(2)}, u32[]{:S(2)}) %all-to-all-start.3) | async-done | bytes 917536 | tf_op jit(solution)/shard_map/all_to_all | solution.py:141
  176.8 1.6 fusion.5
  178.4 1.6 fusion.31
  179.9 1.5 copy.79
  181.5 2.9 convert_element_type.133
  184.4 2.3 convolution_convert_fusion
  186.8 53.2 %all-gather.7.cloned.1.call-done = bf16[640,7168]{1,0:T(8,128)(2,1)} async-done(((bf16[40,7168]{1,0:T(8,128)(2,1)}), bf16[640,7168]{1,0:T(8,128)(2,1)}) %all-gather.7.cloned.1.call-update) | async-done | bytes 9175056 | tf_op jit(solution)/shard_map/all_gather | solution.py:148
  239.9 6.8 %fusion.11 = f32[640,128]{1,0:T(8,128)S(1)} fusion(bf16[640,7168]{1,0:T(8,128)(2,1)} %all-gather.7.cloned.1.call-done, bf16[1,7168,128]{2,1,0:T(8,128)(2,1)} %param.29), kind=kOutput, calls=%fused_computation.17 | convolution fusion | flops 1174405120 | bytes 11337728 | tf_op jit(solution)/shard_map/dot_general | solution.py:149
  247.2 3.2 fusion.23
  251.0 39.7 %all-gather.9.cloned.1.call-done = bf16[10240,128]{1,0:T(8,128)(2,1)} async-done(((bf16[640,128]{1,0:T(8,128)(2,1)}), bf16[10240,128]{1,0:T(8,128)(2,1)}) %all-gather.9.cloned.1.call-update) | async-done | bytes 2621456 | tf_op jit(solution)/shard_map/all_gather | solution.py:152
  290.8 2.9 fusion.19
  294.5 2.4 fusion.17
  298.3 24.5 %all_to_all.44 = bf16[16,40,448]{2,1,0:T(8,128)(2,1)} all-to-all(bf16[16,40,448]{2,1,0:T(8,128)(2,1)S(1)} %bitcast.120), channel_id=1, replica_groups=mesh['role'=2,'dp'=16,'tensor'=8] {'role','tensor'}, dimensions={0} | all-to-all | bytes 1146880 | tf_op jit(solution)/shard_map/all_to_all | solution.py:166
  322.9 6.8 %all-to-all-start.5 = ((bf16[16,40,448]{2,1,0:T(8,128)(2,1)}), bf16[16,40,448]{2,1,0:T(8,128)(2,1)S(1)}, u32[]{:S(2)}, u32[]{:S(2)}) async-start(bf16[16,40,448]{2,1,0:T(8,128)(2,1)} %all_to_all.44), calls=%async_computation.5 | async-start | bytes 1310720 | tf_op jit(solution)/shard_map/all_to_all | solution.py:167
  329.7 12.1 %all-to-all-done.5 = bf16[16,40,448]{2,1,0:T(8,128)(2,1)S(1)} async-done(((bf16[16,40,448]{2,1,0:T(8,128)(2,1)}), bf16[16,40,448]{2,1,0:T(8,128)(2,1)S(1)}, u32[]{:S(2)}, u32[]{:S(2)}) %all-to-all-start.5) | async-done | bytes 573472 | tf_op jit(solution)/shard_map/all_to_all | solution.py:167
  (90 shorter events, 20.3 us)
Async XLA Ops:
  6.5 287.1 %copy-start = (bf16[3,1,64,7168]{3,2,1,0:T(8,128)(2,1)S(1)}, bf16[3,1,64,7168]{3,2,1,0:T(8,128)(2,1)}, u32[]{:S(2)}) copy-start(bf16[3,1,64,7168]{3,2,1,0:T(8,128)(2,1)} %param.33) | copy-start | bytes 8257540
  8.1 5.0 %slice-start = ((s8[4718592]{0:T(1024)(128)(4,1)}), s8[4194304]{0:T(1024)(128)(4,1)S(1)}, s32[]{:S(2)}) async-start(s8[4718592]{0:T(1024)(128)(4,1)} %bitcast.118), calls=%async_computation.9 | async-start | bytes 8388608
  8.1 4.0 %copy-start.5 = (bf16[8,64,576]{2,1,0:T(8,128)(2,1)S(1)}, bf16[8,64,576]{2,1,0:T(8,128)(2,1)}, u32[]{:S(2)}) copy-start(bf16[8,64,576]{2,1,0:T(8,128)(2,1)} %param.18) | copy-start | bytes 1769476
  8.2 5.0 %slice-start.1 = ((s8[4718592]{0:T(1024)(128)(4,1)}), s8[524288]{0:T(1024)(128)(4,1)S(1)}, s32[]{:S(2)}) async-start(s8[4718592]{0:T(1024)(128)(4,1)} %bitcast.118), calls=%async_computation.10 | async-start | bytes 1048576
  13.2 2.5 copy-start.10
  15.8 11.3 %copy-start.11 = (s32[64,8]{0,1:T(8,128)S(1)}, s32[64,8]{0,1:T(8,128)}, u32[]{:S(2)}) copy-start(s32[64,8]{0,1:T(8,128)} %param.26) | copy-start | bytes 6148
  17.4 10.1 %copy-start.15 = (s32[64]{0:T(128)S(1)}, s32[64]{0:T(128)}, u32[]{:S(2)}) copy-start(s32[64]{0:T(128)} %param.28) | copy-start | bytes 772
  18.5 24.6 %all-to-all-start.1 = ((bf16[8,64,512]{2,0,1:T(8,128)(2,1)}), bf16[8,64,512]{2,0,1:T(8,128)(2,1)S(1)}, u32[]{:S(2)}, u32[]{:S(2)}) async-start(bf16[8,64,512]{2,0,1:T(8,128)(2,1)} %copy.75), calls=%async_computation.1 | async-start | bytes 1048576 | tf_op jit(solution)/shard_map/all_to_all | solution.py:107
  27.1 4.5 %copy-start.9 = (bf16[3,1,128,64]{2,3,1,0:T(8,128)(2,1)S(1)}, bf16[3,1,128,64]{2,3,1,0:T(8,128)(2,1)}, u32[]{:S(2)}) copy-start(bf16[3,1,128,64]{2,3,1,0:T(8,128)(2,1)} %param.32) | copy-start | bytes 147460
  31.6 1.5 copy-start.1
  43.1 70.1 %all-to-all-start = ((bf16[16,136,640]{2,1,0:T(8,128)(2,1)}), bf16[16,136,640]{2,1,0:T(8,128)(2,1)}, u32[]{:S(2)}, u32[]{:S(2)}) async-start(bf16[16,136,640]{2,1,0:T(8,128)(2,1)} %copy.72), calls=%async_computation | async-start | bytes 5570560 | tf_op jit(solution)/shard_map/all_to_all | solution.py:70
  50.1 71.1 %all-gather.5.cloned.1.call-start = ((), (), s32[]{:S(2)}) async-start(), calls=%async_computation.6 | async-start | bytes 2228224 | tf_op jit(solution)/shard_map/all_gather | solution.py:114
  124.2 1.3 copy-start.3
  125.5 2.1 collective-permute-start
  126.0 26.9 %copy-start.8 = (bf16[64,448]{1,0:T(8,128)(2,1)S(1)}, bf16[64,448]{1,0:T(8,128)(2,1)}, u32[]{:S(2)}) copy-start(bf16[64,448]{1,0:T(8,128)(2,1)} %param.24) | copy-start | bytes 172036
  152.8 9.2 %copy-start.13 = (bf16[7168]{0:T(1024)(128)(2,1)S(1)}, bf16[7168]{0:T(1024)(128)(2,1)}, u32[]{:S(2)}) copy-start(bf16[7168]{0:T(1024)(128)(2,1)} %param.25) | copy-start | bytes 43012
  152.9 0.6 copy-start.6
  154.6 22.2 %all-to-all-start.3 = ((bf16[16,64,448]{2,1,0:T(8,128)(2,1)}), bf16[16,64,448]{2,1,0:T(8,128)(2,1)}, u32[]{:S(2)}, u32[]{:S(2)}) async-start(bf16[16,64,448]{2,1,0:T(8,128)(2,1)} %broadcast_in_dim.39), calls=%async_computation.3 | async-start | bytes 2097152 | tf_op jit(solution)/shard_map/all_to_all | solution.py:141
  161.7 78.2 %all-gather.7.cloned.1.call-start = ((), (), s32[]{:S(2)}) async-start(), calls=%async_computation.7 | async-start | bytes 9748480 | tf_op jit(solution)/shard_map/all_gather | solution.py:148
  186.7 104.0 %all-gather.9.cloned.1.call-start = ((), (), s32[]{:S(2)}) async-start(), calls=%async_computation.8 | async-start | bytes 2785280 | tf_op jit(solution)/shard_map/all_gather | solution.py:152
  239.9 6.8 %copy-start.16 = (bf16[640,7168]{1,0:T(8,128)(2,1)S(1)}, bf16[640,7168]{1,0:T(8,128)(2,1)}, u32[]{:S(2)}) copy-start(bf16[640,7168]{1,0:T(8,128)(2,1)} %all-gather.7.cloned.1.call-done) | copy-start | bytes 27525124
  239.9 7.2 %copy-start.18 = (bf16[1,7168,128]{2,1,0:T(8,128)(2,1)S(1)}, bf16[1,7168,128]{2,1,0:T(8,128)(2,1)}, u32[]{:S(2)}) copy-start(bf16[1,7168,128]{2,1,0:T(8,128)(2,1)} %param.30) | copy-start | bytes 5505028
  247.2 43.6 %copy-start.4 = (bf16[2048,192]{0,1:T(8,128)(2,1)S(1)}, bf16[2048,192]{0,1:T(8,128)(2,1)}, u32[]{:S(2)}) copy-start(bf16[2048,192]{0,1:T(8,128)(2,1)} %copy.73) | copy-start | bytes 2359300
  290.8 3.8 %copy-start.2 = (bf16[2048,448]{1,0:T(8,128)(2,1)S(1)}, bf16[2048,448]{1,0:T(8,128)(2,1)}, u32[]{:S(2)}) copy-start(bf16[2048,448]{1,0:T(8,128)(2,1)} %slice.41) | copy-start | bytes 5505028
  290.8 3.8 %copy-start.17 = (bf16[10240,128]{1,0:T(8,128)(2,1)S(1)}, bf16[10240,128]{1,0:T(8,128)(2,1)}, u32[]{:S(2)}) copy-start(bf16[10240,128]{1,0:T(8,128)(2,1)} %all-gather.9.cloned.1.call-done) | copy-start | bytes 7864324
  297.0 32.7 %copy-start.12 = (s32[64,8]{0,1:T(8,128)S(1)}, s32[64,8]{0,1:T(8,128)}, u32[]{:S(2)}) copy-start(s32[64,8]{0,1:T(8,128)} %param.26) | copy-start | bytes 6148
  297.0 32.7 %copy-start.14 = (f32[64,8]{0,1:T(8,128)S(1)}, f32[64,8]{0,1:T(8,128)}, u32[]{:S(2)}) copy-start(f32[64,8]{0,1:T(8,128)} %param.27) | copy-start | bytes 6148
  297.0 44.9 %copy-start.7 = (bf16[64,448]{1,0:T(8,128)(2,1)S(1)}, bf16[64,448]{1,0:T(8,128)(2,1)}, u32[]{:S(2)}) copy-start(bf16[64,448]{1,0:T(8,128)(2,1)} %copy-done.6) | copy-start | bytes 172036
  322.9 19.0 %all-to-all-start.5 = ((bf16[16,40,448]{2,1,0:T(8,128)(2,1)}), bf16[16,40,448]{2,1,0:T(8,128)(2,1)S(1)}, u32[]{:S(2)}, u32[]{:S(2)}) async-start(bf16[16,40,448]{2,1,0:T(8,128)(2,1)} %all_to_all.44), calls=%async_computation.5 | async-start | bytes 1310720 | tf_op jit(solution)/shard_map/all_to_all | solution.py:167
Sparse Core Ops, SparseCore 0:
  53.3 51.1 all-gather.4
  186.8 53.0 all-gather.6
  250.5 40.1 all-gather.8
where the time goes:
time: 351 us; the launch traced here: 350 us
  waiting for transfers between devices  183 us (52%)
  blocking collectives  46.3 us (13%)
  matrix products  32.5 us (9%)
  local copies, waits for them, and re-layouts  32.1 us (9%)
  starting transfers between devices  30.2 us (9%)
  between operations  13.5 us (4%)
  other arithmetic  12.3 us (4%)
    all_to_all x1, waiting for transfers between devices, local(): lax.all_to_all(down_pack, RT, split_axis=0, concat_axis=0, tiled=True)  60.9 us
    all_gather x1, waiting for transfers between devices, local(): collected_rows = lax.all_gather(picked, RT, axis=0, tiled=True)  53.2 us
    all_gather x1, waiting for transfers between devices, local(): gathered = lax.all_gather(hidden, RT, axis=0, tiled=False)  39.7 us
    all_to_all x1, blocking collectives, local(): lax.all_to_all(expert_out, RT, split_axis=0, concat_axis=0, tiled=True)  24.5 us
    all_to_all x1, blocking collectives, local(): lax.all_to_all(partial.astype(jnp.bfloat16), 'tensor', split_axis=0, conc...  21.8 us
    all_to_all x1, waiting for transfers between devices, local(): lax.all_to_all(spread, 'dp', split_axis=0, concat_axis=0, tiled=True)  14.8 us
    all_to_all x1, waiting for transfers between devices, local(): lax.all_to_all(by_group, 'dp', split_axis=0, concat_axis=0, tiled=True)  12.1 us
    all_to_all x1, starting transfers between devices, local(): lax.all_to_all(attended, 'tensor', split_axis=1, concat_axis=0, tiled=True)  8.57 us
  transfers between devices with their start and end apart: 8, of which 7 were waited for; matrix products, arithmetic and copies ran while one was open for 7% of the time, Pallas kernels for 0%

commit v1 on v0

--- a/solution.py
+++ b/solution.py
@@ -145,7 +145,9 @@
     picked = jnp.dot(mine.astype(jnp.bfloat16), normed, preferred_element_type=jnp.float32).astype(
         jnp.bfloat16
     )
-    collected_rows = lax.all_gather(picked, RT, axis=0, tiled=True)
+    collected_rows = jnp.concatenate(
+        jax.lax.all_to_all(jnp.stack([picked] * jax.lax.axis_size(RT), 0), RT, 0, 0), 0
+    )
     gate_scores = jnp.dot(collected_rows, expert_gate_weight[0], preferred_element_type=jnp.float32)
     upper_bound = jnp.dot(collected_rows, expert_up_weight[0], preferred_element_type=jnp.float32)
     hidden = (jax.nn.silu(gate_scores) * upper_bound).astype(jnp.bfloat16)

time: 351 us -> 494 us (1.41)
  blocking collectives: 46.3 us -> 253 us
  waiting for transfers between devices: 183 us -> 123 us
  matrix products: 32.5 us -> 27.4 us
    all_to_all x0 -> x1, blocking collectives: none -> 207 us  [local(): jax.lax.all_to_all(jnp.stack([picked] * jax.lax.axis_size(RT), 0), RT, 0, 0)]
    all_gather x1 -> x0, waiting for transfers between devices: 53.2 us -> none  [local(): collected_rows = lax.all_gather(picked, RT, axis=0, tiled=True)]
    all_gather x1, waiting for transfers between devices: 39.7 us -> 33.6 us  [local(): gathered = lax.all_gather(hidden, RT, axis=0, tiled=False)]
  transfers between devices with their start and end apart: 8 -> 7, of which waited for: 7 -> 6; matrix products, arithmetic and copies ran while one was open for 7% -> 5% of each run, Pallas kernels for 0% -> 0%
where the time goes in v1:
time: 494 us; the launch traced here: 493 us
  blocking collectives  253 us (51%)
  waiting for transfers between devices  123 us (25%)
  local copies, waits for them, and re-layouts  32.9 us (7%)
  starting transfers between devices  30.1 us (6%)
  matrix products  27.4 us (6%)
  between operations  13.8 us (3%)
  other arithmetic  12.3 us (2%)
    all_to_all x1, blocking collectives, local(): jax.lax.all_to_all(jnp.stack([picked] * jax.lax.axis_size(RT), 0), RT, 0, 0)  207 us
    all_to_all x1, waiting for transfers between devices, local(): lax.all_to_all(down_pack, RT, split_axis=0, concat_axis=0, tiled=True)  60.9 us
    all_gather x1, waiting for transfers between devices, local(): gathered = lax.all_gather(hidden, RT, axis=0, tiled=False)  33.6 us
    all_to_all x1, blocking collectives, local(): lax.all_to_all(expert_out, RT, split_axis=0, concat_axis=0, tiled=True)  24.5 us
    all_to_all x1, blocking collectives, local(): lax.all_to_all(partial.astype(jnp.bfloat16), 'tensor', split_axis=0, conc...  21.8 us
    all_to_all x1, waiting for transfers between devices, local(): lax.all_to_all(spread, 'dp', split_axis=0, concat_axis=0, tiled=True)  14.8 us
    all_to_all x1, waiting for transfers between devices, local(): lax.all_to_all(by_group, 'dp', split_axis=0, concat_axis=0, tiled=True)  12.1 us
  transfers between devices with their start and end apart: 7, of which 6 were waited for; matrix products, arithmetic and copies ran while one was open for 5% of the time, Pallas kernels for 0%

profile of v1, /device:TPU:32, one launch (start us, length us, event | category | flops | bytes accessed | tf_op | source)
XLA Modules:
  0.0 493.3 jit_solution(2510581231008487154)
XLA Ops:
  8.2 3.9 fusion.8
  13.2 2.5 fusion.2
  15.8 1.6 fusion.18
  18.5 8.6 %all-to-all-start.1 = ((bf16[8,64,512]{2,0,1:T(8,128)(2,1)}), bf16[8,64,512]{2,0,1:T(8,128)(2,1)S(1)}, u32[]{:S(2)}, u32[]{:S(2)}) async-start(bf16[8,64,512]{2,0,1:T(8,128)(2,1)} %copy.75), calls=%async_computation.1 | async-start | bytes 1048576 | tf_op jit(solution)/shard_map/all_to_all | solution.py:107
  27.6 3.9 copy.70
  33.0 3.5 pad_maximum_fusion
  36.5 6.2 %copy.72 = bf16[16,136,640]{2,1,0:T(8,128)(2,1)} copy(bf16[16,136,640]{1,2,0:T(8,128)(2,1)} %pad_maximum_fusion) | data formatting | bytes 5570560 | tf_op jit(solution)/shard_map/concatenate | solution.py:69
  43.1 6.9 %all-to-all-start = ((bf16[16,136,640]{2,1,0:T(8,128)(2,1)}), bf16[16,136,640]{2,1,0:T(8,128)(2,1)}, u32[]{:S(2)}, u32[]{:S(2)}) async-start(bf16[16,136,640]{2,1,0:T(8,128)(2,1)} %copy.72), calls=%async_computation | async-start | bytes 5570560 | tf_op jit(solution)/shard_map/all_to_all | solution.py:70
  50.0 1.5 fusion.27
  52.3 60.9 %all-to-all-done = bf16[16,136,640]{2,1,0:T(8,128)(2,1)} async-done(((bf16[16,136,640]{2,1,0:T(8,128)(2,1)}), bf16[16,136,640]{2,1,0:T(8,128)(2,1)}, u32[]{:S(2)}, u32[]{:S(2)}) %all-to-all-start) | async-done | bytes 2785312 | tf_op jit(solution)/shard_map/all_to_all | solution.py:70
  113.2 2.0 slice.40
  116.6 1.5 slice.42
  118.2 2.2 copy.73
  121.3 3.0 fusion.63
  126.1 1.6 collective-permute-done
  127.6 2.2 add_convert_fusion
  131.1 21.8 %all_to_all.48 = bf16[8,64,448]{2,1,0:T(8,128)(2,1)S(1)} all-to-all(bf16[8,64,448]{2,1,0:T(8,128)(2,1)S(1)} %bitcast.126), channel_id=1, replica_groups=mesh['role'=2,'dp'=16,'tensor'=8] {'tensor'}, dimensions={0} | all-to-all | bytes 917504 | tf_op jit(solution)/shard_map/all_to_all | solution.py:132
  154.7 7.1 %all-to-all-start.3 = ((bf16[16,64,448]{2,1,0:T(8,128)(2,1)}), bf16[16,64,448]{2,1,0:T(8,128)(2,1)}, u32[]{:S(2)}, u32[]{:S(2)}) async-start(bf16[16,64,448]{2,1,0:T(8,128)(2,1)} %broadcast_in_dim.39), calls=%async_computation.3 | async-start | bytes 2097152 | tf_op jit(solution)/shard_map/all_to_all | solution.py:141
  162.1 14.8 %all-to-all-done.3 = bf16[16,64,448]{2,1,0:T(8,128)(2,1)} async-done(((bf16[16,64,448]{2,1,0:T(8,128)(2,1)}), bf16[16,64,448]{2,1,0:T(8,128)(2,1)}, u32[]{:S(2)}, u32[]{:S(2)}) %all-to-all-start.3) | async-done | bytes 917536 | tf_op jit(solution)/shard_map/all_to_all | solution.py:141
  176.9 1.6 fusion.5
  178.5 1.6 fusion.31
  180.0 1.6 copy.79
  181.6 2.9 convert_element_type.133
  187.1 207.1 %all_to_all.49 = bf16[16,40,7168]{2,1,0:T(8,128)(2,1)S(1)} all-to-all(bf16[16,40,7168]{2,1,0:T(8,128)(2,1)S(1)} %stack.2), channel_id=1, replica_groups=mesh['role'=2,'dp'=16,'tensor'=8] {'role','tensor'}, dimensions={0} | all-to-all | bytes 18350080 | tf_op jit(solution)/shard_map/all_to_all | solution.py:149
  394.2 2.5 fusion.11
  396.8 3.2 fusion.23
  400.6 33.6 %all-gather.6.cloned.1.call-done = bf16[10240,128]{1,0:T(8,128)(2,1)} async-done(((bf16[640,128]{1,0:T(8,128)(2,1)}), bf16[10240,128]{1,0:T(8,128)(2,1)}) %all-gather.6.cloned.1.call-update) | async-done | bytes 2621456 | tf_op jit(solution)/shard_map/all_gather | solution.py:154
  434.2 2.9 fusion.19
  438.0 2.4 fusion.17
  441.8 24.5 %all_to_all.50 = bf16[16,40,448]{2,1,0:T(8,128)(2,1)} all-to-all(bf16[16,40,448]{2,1,0:T(8,128)(2,1)S(1)} %bitcast.123), channel_id=1, replica_groups=mesh['role'=2,'dp'=16,'tensor'=8] {'role','tensor'}, dimensions={0} | all-to-all | bytes 1146880 | tf_op jit(solution)/shard_map/all_to_all | solution.py:168
  466.3 6.8 %all-to-all-start.6 = ((bf16[16,40,448]{2,1,0:T(8,128)(2,1)}), bf16[16,40,448]{2,1,0:T(8,128)(2,1)S(1)}, u32[]{:S(2)}, u32[]{:S(2)}) async-start(bf16[16,40,448]{2,1,0:T(8,128)(2,1)} %all_to_all.50), calls=%async_computation.6 | async-start | bytes 1310720 | tf_op jit(solution)/shard_map/all_to_all | solution.py:169
  473.2 12.1 %all-to-all-done.6 = bf16[16,40,448]{2,1,0:T(8,128)(2,1)S(1)} async-done(((bf16[16,40,448]{2,1,0:T(8,128)(2,1)}), bf16[16,40,448]{2,1,0:T(8,128)(2,1)S(1)}, u32[]{:S(2)}, u32[]{:S(2)}) %all-to-all-start.6) | async-done | bytes 573472 | tf_op jit(solution)/shard_map/all_to_all | solution.py:169
  (89 shorter events, 21.0 us)
Async XLA Ops:
  6.5 430.6 %copy-start = (bf16[3,1,64,7168]{3,2,1,0:T(8,128)(2,1)S(1)}, bf16[3,1,64,7168]{3,2,1,0:T(8,128)(2,1)}, u32[]{:S(2)}) copy-start(bf16[3,1,64,7168]{3,2,1,0:T(8,128)(2,1)} %param.33) | copy-start | bytes 8257540
  8.1 5.0 %slice-start = ((s8[4718592]{0:T(1024)(128)(4,1)}), s8[4194304]{0:T(1024)(128)(4,1)S(1)}, s32[]{:S(2)}) async-start(s8[4718592]{0:T(1024)(128)(4,1)} %bitcast.121), calls=%async_computation.9 | async-start | bytes 8388608
  8.1 4.0 copy-start.5
  8.2 5.0 %slice-start.1 = ((s8[4718592]{0:T(1024)(128)(4,1)}), s8[524288]{0:T(1024)(128)(4,1)S(1)}, s32[]{:S(2)}) async-start(s8[4718592]{0:T(1024)(128)(4,1)} %bitcast.121), calls=%async_computation.10 | async-start | bytes 1048576
  13.2 2.5 copy-start.10
  15.8 11.3 %copy-start.11 = (s32[64,8]{0,1:T(8,128)S(1)}, s32[64,8]{0,1:T(8,128)}, u32[]{:S(2)}) copy-start(s32[64,8]{0,1:T(8,128)} %param.26) | copy-start | bytes 6148
  17.4 10.0 %copy-start.15 = (s32[64]{0:T(128)S(1)}, s32[64]{0:T(128)}, u32[]{:S(2)}) copy-start(s32[64]{0:T(128)} %param.28) | copy-start | bytes 772
  18.5 24.6 %all-to-all-start.1 = ((bf16[8,64,512]{2,0,1:T(8,128)(2,1)}), bf16[8,64,512]{2,0,1:T(8,128)(2,1)S(1)}, u32[]{:S(2)}, u32[]{:S(2)}) async-start(bf16[8,64,512]{2,0,1:T(8,128)(2,1)} %copy.75), calls=%async_computation.1 | async-start | bytes 1048576 | tf_op jit(solution)/shard_map/all_to_all | solution.py:107
  27.1 4.5 copy-start.9
  31.5 1.5 copy-start.1
  43.1 70.1 %all-to-all-start = ((bf16[16,136,640]{2,1,0:T(8,128)(2,1)}), bf16[16,136,640]{2,1,0:T(8,128)(2,1)}, u32[]{:S(2)}, u32[]{:S(2)}) async-start(bf16[16,136,640]{2,1,0:T(8,128)(2,1)} %copy.72), calls=%async_computation | async-start | bytes 5570560 | tf_op jit(solution)/shard_map/all_to_all | solution.py:70
  50.0 71.3 %all-gather.4.cloned.1.call-start = ((), (), s32[]{:S(2)}) async-start(), calls=%async_computation.7 | async-start | bytes 2228224 | tf_op jit(solution)/shard_map/all_gather | solution.py:114
  124.3 1.3 copy-start.3
  125.6 2.1 collective-permute-start
  126.1 26.9 %copy-start.8 = (bf16[64,448]{1,0:T(8,128)(2,1)S(1)}, bf16[64,448]{1,0:T(8,128)(2,1)}, u32[]{:S(2)}) copy-start(bf16[64,448]{1,0:T(8,128)(2,1)} %param.24) | copy-start | bytes 172036
  152.9 9.1 %copy-start.13 = (bf16[7168]{0:T(1024)(128)(2,1)S(1)}, bf16[7168]{0:T(1024)(128)(2,1)}, u32[]{:S(2)}) copy-start(bf16[7168]{0:T(1024)(128)(2,1)} %param.25) | copy-start | bytes 43012
  153.0 0.6 copy-start.6
  154.7 22.2 %all-to-all-start.3 = ((bf16[16,64,448]{2,1,0:T(8,128)(2,1)}), bf16[16,64,448]{2,1,0:T(8,128)(2,1)}, u32[]{:S(2)}, u32[]{:S(2)}) async-start(bf16[16,64,448]{2,1,0:T(8,128)(2,1)} %broadcast_in_dim.39), calls=%async_computation.3 | async-start | bytes 2097152 | tf_op jit(solution)/shard_map/all_to_all | solution.py:141
  161.8 272.4 %all-gather.6.cloned.1.call-start = ((), (), s32[]{:S(2)}) async-start(), calls=%async_computation.8 | async-start | bytes 2785280 | tf_op jit(solution)/shard_map/all_gather | solution.py:154
  187.1 207.1 %copy-start.17 = (bf16[1,7168,128]{2,1,0:T(8,128)(2,1)S(1)}, bf16[1,7168,128]{2,1,0:T(8,128)(2,1)}, u32[]{:S(2)}) copy-start(bf16[1,7168,128]{2,1,0:T(8,128)(2,1)} %param.29) | copy-start | bytes 5505028
  394.2 2.5 copy-start.18
  396.8 37.4 %copy-start.4 = (bf16[2048,192]{0,1:T(8,128)(2,1)S(1)}, bf16[2048,192]{0,1:T(8,128)(2,1)}, u32[]{:S(2)}) copy-start(bf16[2048,192]{0,1:T(8,128)(2,1)} %copy.73) | copy-start | bytes 2359300
  434.2 3.8 copy-start.2
  434.2 3.8 copy-start.16
  440.5 32.7 %copy-start.12 = (s32[64,8]{0,1:T(8,128)S(1)}, s32[64,8]{0,1:T(8,128)}, u32[]{:S(2)}) copy-start(s32[64,8]{0,1:T(8,128)} %param.26) | copy-start | bytes 6148
  440.5 32.7 %copy-start.14 = (f32[64,8]{0,1:T(8,128)S(1)}, f32[64,8]{0,1:T(8,128)}, u32[]{:S(2)}) copy-start(f32[64,8]{0,1:T(8,128)} %param.27) | copy-start | bytes 6148
  440.5 44.9 %copy-start.7 = (bf16[64,448]{1,0:T(8,128)(2,1)S(1)}, bf16[64,448]{1,0:T(8,128)(2,1)}, u32[]{:S(2)}) copy-start(bf16[64,448]{1,0:T(8,128)(2,1)} %copy-done.6) | copy-start | bytes 172036
  466.3 19.0 %all-to-all-start.6 = ((bf16[16,40,448]{2,1,0:T(8,128)(2,1)}), bf16[16,40,448]{2,1,0:T(8,128)(2,1)S(1)}, u32[]{:S(2)}, u32[]{:S(2)}) async-start(bf16[16,40,448]{2,1,0:T(8,128)(2,1)} %all_to_all.50), calls=%async_computation.6 | async-start | bytes 1310720 | tf_op jit(solution)/shard_map/all_to_all | solution.py:169
Sparse Core Ops, SparseCore 0:
  53.2 51.1 all-gather.3
  400.1 34.0 all-gather.5
